TPU v7x, 128 devices: a whole 4x4x4 slice. The times are simulated.
128 devices in a mesh: row: 8 (over x, y_hi), col: 16 (over y_lo, z, core).
Axes of the slice: x: 4, y: 4 (y_hi: 2, y_lo: 2; y = y_hi * 2 + y_lo), z: 4, core: 2. Of those that a mesh axis runs over, the one named last changes fastest.
Arguments:
- flat_gradient: bfloat16 [8, 16, 524288], P('row', 'col'), may hold values from -6 to 6
- range_rows: int32 [8, 16], replicated, may hold values from 1 to 64, 512 in all within a row
- left_stat: float32 [4096, 4096], P('row', 'col'), may hold values from -6 to 6
- right_stat: float32 [8192, 8192], P('col', 'row'), may hold values from -6 to 6
- left_root: bfloat16 [4096, 4096], P('row'), as said below
- right_root: bfloat16 [8192, 8192], P('col'), as said below
Outputs:
- left_new: float32 [4096, 4096], P('row', 'col')
- right_new: float32 [8192, 8192], P('col', 'row')
- update: bfloat16 [4096, 8192], P('row', 'col')
Inputs may be any that keep to these rules, and one draw needn't show every extreme that they name: In each row r the entries sum to 512; the largest entry of every row is exactly 64. Slots of flat_gradient beyond a device's range_rows rows are padding. left_root equals its transpose. right_root equals its transpose.
All inputs are finite; a program needn't handle non-finite values.
Results may differ from a plain program's by a relative error of at most 0.014.
Values may be sent and summed in bfloat16 or wider, within the bound.
No kernel may reach another device: no remote copies, remote signals or barrier semaphores. Data moves between devices by JAX's collectives and lax.ppermute only.
A program may use at most 192 MiB of HBM per device.

v0:
```python
import math
import jax
import jax.numpy as jnp
from jax import lax
from jax.sharding import PartitionSpec as P

HQ = 4096
DIN = 8192
stat_decay = 0.9


def shifted(block, axis, distance):
    devices = range(lax.axis_size(axis))
    route = [((i - distance) % len(devices), i) for i in devices]
    return lax.ppermute(block, axis, route)


def broadcast(block, axis, source):
    block = jnp.where(lax.axis_index(axis) == source, block, jnp.zeros_like(block))
    return lax.psum(block, axis)


def slot_index(row_counts, tile_rows, capacity):
    offsets = jnp.cumsum(row_counts) - row_counts
    target = jnp.arange(tile_rows, dtype=jnp.int32)
    covered = target[:, None] >= offsets[None, :]
    source = jnp.sum(covered.astype(jnp.int32), axis=1) - 1
    begins = jnp.max(jnp.where(covered, offsets[None, :], 0), axis=1)
    return source * capacity + target - begins


def shards(flat_gradient, range_rows, left_stat, right_stat, left_root, right_root):
    row_count = lax.axis_size("row")
    col_count = lax.axis_size("col")
    row_index = lax.axis_index("row")
    tile_rows = HQ // row_count
    capacity = flat_gradient.shape[2] // DIN
    held_rows = flat_gradient.reshape(capacity, DIN)
    received = lax.all_to_all(held_rows, "col", split_axis=1, concat_axis=0, tiled=True)
    row_counts = lax.dynamic_index_in_dim(range_rows, row_index, 0, keepdims=False)
    grad_tile = jnp.take(received, slot_index(row_counts, tile_rows, capacity), axis=0)
    column_panel = lax.all_gather(grad_tile, "row", axis=0, tiled=True)
    half_count = row_count // 2
    rotated = jnp.roll(column_panel, -row_index * tile_rows, axis=0)
    upper_part = lax.dot_general(
        grad_tile,
        rotated[: (half_count + 1) * tile_rows],
        (((1,), (1,)), ((), ())),
        preferred_element_type=jnp.float32,
    )
    upper_blocks = [
        upper_part[:, stride * tile_rows : (stride + 1) * tile_rows]
        for stride in range(half_count + 1)
    ]
    mirrored = {}
    for stride in range(1, half_count):
        mirrored[stride] = shifted(
            upper_blocks[stride].T.astype(jnp.bfloat16), "row", stride
        ).astype(jnp.float32)
    all_blocks = upper_blocks + [
        mirrored[row_count - distance] for distance in range(half_count + 1, row_count)
    ]
    left_part = jnp.roll(jnp.concatenate(all_blocks, axis=1), row_index * tile_rows, axis=1)
    left_sum = lax.psum_scatter(
        left_part.astype(jnp.bfloat16), "col", scatter_dimension=1, tiled=True
    ).astype(jnp.float32)
    panel_ratio = col_count // row_count
    partner_list = []
    for member in range(panel_ratio):
        partner_list.append(broadcast(column_panel, "col", row_index * panel_ratio + member))
    partner_panel = jnp.concatenate(partner_list, axis=1)
    right_gram = lax.dot_general(
        column_panel, partner_panel, (((0,), (0,)), ((), ())), preferred_element_type=jnp.float32
    )
    right_new = stat_decay * right_stat + right_gram * (1.0 / math.sqrt(HQ))
    left_mixed = jnp.dot(left_root, column_panel, preferred_element_type=jnp.float32).astype(
        jnp.bfloat16
    )
    update_sum = lax.dot_general(
        lax.all_gather(left_mixed, "col", axis=1, tiled=True),
        right_root,
        (((1,), (1,)), ((), ())),
        preferred_element_type=jnp.float32,
    )
    left_new = stat_decay * left_stat + left_sum * (1.0 / math.sqrt(DIN))
    return (left_new, right_new, update_sum.astype(jnp.bfloat16))


def solution(mesh):
    in_specs = (
        P("row", "col", None),
        P(),
        P("row", "col"),
        P("col", "row"),
        P("row", None),
        P("col", None),
    )
    out_specs = (P("row", "col"), P("col", "row"), P("row", "col"))
    return jax.shard_map(shards, mesh=mesh, in_specs=in_specs, out_specs=out_specs, check_vma=False)
```

profile of v0, /device:TPU:1, one launch (start us, length us, event | category | flops | bytes accessed | tf_op | source)
XLA Modules:
  0.0 440.1 jit_solution(12549819292666009770)
XLA Ops:
  7.2 22.8 %reduce = bf16[524288]{0:T(1024)(128)(2,1)S(1)} reduce(bf16[1,1,524288]{2,1,0:T(2,128)(2,1)} %param.6, bf16[]{:T(256)} %constant.91), dimensions={0,1}, to_apply=%param.6.reduce_sub_computation | reduce | bytes 2097154 | tf_op args[0]
  30.6 1.5 copy.13
  32.2 7.8 %all-to-all-start = ((bf16[64,16,512]{2,0,1:T(8,128)(2,1)}), bf16[64,16,512]{2,0,1:T(8,128)(2,1)S(1)}, u32[]{:S(2)}, u32[]{:S(2)}) async-start(bf16[64,16,512]{2,0,1:T(8,128)(2,1)} %copy.13), calls=%async_computation | async-start | bytes 2097152 | tf_op jit(solution)/shard_map/all_to_all | solution.py:39
  41.8 14.0 %all-to-all-done = bf16[64,16,512]{2,0,1:T(8,128)(2,1)S(1)} async-done(((bf16[64,16,512]{2,0,1:T(8,128)(2,1)}), bf16[64,16,512]{2,0,1:T(8,128)(2,1)S(1)}, u32[]{:S(2)}, u32[]{:S(2)}) %all-to-all-start) | async-done | bytes 1048608 | tf_op jit(solution)/shard_map/all_to_all | solution.py:39
  55.9 2.0 gather_fusion
  57.8 0.9 broadcast_select_fusion.2
  58.8 70.9 %all-gather.3.cloned.1.call-done = bf16[4096,512]{1,0:T(8,128)(2,1)} async-done(((bf16[512,512]{1,0:T(8,128)(2,1)}), bf16[4096,512]{1,0:T(8,128)(2,1)}) %all-gather.3.cloned.1.call-update) | async-done | bytes 4194320 | tf_op jit(solution)/shard_map/all_gather | solution.py:42
  129.7 6.0 %broadcast_select_fusion.1 = (bf16[4096,512]{1,0:T(8,128)(2,1)}, bf16[4096,512]{1,0:T(8,128)(2,1)}) fusion(bf16[4096,512]{1,0:T(8,128)(2,1)} %all-gather.3.cloned.1.call-done, pred[]{:T(512)S(6)} %eq.11, pred[]{:T(512)S(6)} %eq.12), kind=kLoop, calls=%fused_computation.9 | loop fusion | flops 4194304 | bytes 12582914 | tf_op jit(solution)/shard_map/jit(_where)/select_n | solution.py:19
  135.8 0.9 copy-done
  136.8 5.1 %constant_dynamic-update-slice_fusion.1 = (bf16[512,8192]{1,0:T(8,128)(2,1)}, bf16[512,2560]{1,0:T(8,128)(2,1)S(1)}) fusion(bf16[512,512]{1,0:T(8,128)(2,1)S(1)} %copy-done, s32[]{:T(128)S(6)} %select_n.71, bf16[4096,512]{1,0:T(8,128)(2,1)} %all-gather.3.cloned.1.call-done), kind=kOutput, calls=%fused_computation.31 | convolution fusion | flops 1347420160 | bytes 9961476 | tf_op jit(solution)/shard_map/dot_general | solution.py:45
  141.9 2.7 copy.14
  144.6 2.5 slice_bitcast_fusion
  147.1 0.8 collective-permute-start.1
  147.9 3.2 collective-permute-start.2
  151.1 12.5 %collective-permute-done = bf16[512,512]{1,0:T(8,128)(2,1)S(1)} collective-permute-done((bf16[512,512]{1,0:T(8,128)(2,1)}, bf16[512,512]{1,0:T(8,128)(2,1)S(1)}, u32[]{:S(2)}, u32[]{:S(2)}) %collective-permute-start) | collective-permute-done | bytes 524320 | tf_op jit(solution)/shard_map/ppermute | solution.py:15
  163.6 0.9 convert_dynamic-update-slice_fusion.4
  164.5 7.7 %collective-permute-done.1 = bf16[512,512]{1,0:T(8,128)(2,1)} collective-permute-done((bf16[512,512]{1,0:T(8,128)(2,1)}, bf16[512,512]{1,0:T(8,128)(2,1)}, u32[]{:S(2)}, u32[]{:S(2)}) %collective-permute-start.1) | collective-permute-done | bytes 524320 | tf_op jit(solution)/shard_map/ppermute | solution.py:15
  172.2 1.9 convert_dynamic-update-slice_fusion.2
  174.1 13.5 %collective-permute-done.2 = bf16[512,512]{1,0:T(8,128)(2,1)S(1)} collective-permute-done((bf16[512,512]{1,0:T(8,128)(2,1)}, bf16[512,512]{1,0:T(8,128)(2,1)S(1)}, u32[]{:S(2)}, u32[]{:S(2)}) %collective-permute-start.2) | collective-permute-done | bytes 524320 | tf_op jit(solution)/shard_map/ppermute | solution.py:15
  187.6 0.8 convert_dynamic-update-slice_fusion
  188.4 1.7 constant_dynamic-update-slice_fusion
  190.1 0.9 convert_dynamic-update-slice_fusion.5
  191.0 2.0 convert_dynamic-update-slice_fusion.3
  193.0 0.9 convert_dynamic-update-slice_fusion.1
  193.9 4.7 %dynamic-slice_convert_fusion = bf16[512,4096]{1,0:T(8,128)(2,1)} fusion(bf16[512,8192]{1,0:T(8,128)(2,1)} %convert_dynamic-update-slice_fusion.1, s32[]{:T(128)S(6)} %select_n.73), kind=kLoop, calls=%fused_computation.7 | loop fusion | bytes 8388612 | tf_op jit(solution)/shard_map/convert_element_type | solution.py:65
  198.6 6.9 %fusion.9 = bf16[512,512]{0,1:T(8,128)(2,1)} fusion(bf16[4096,512]{1,0:T(8,128)(2,1)} %all-gather.3.cloned.1.call-done, bf16[512,4096]{1,0:T(8,128)(2,1)} %param.10), kind=kOutput, calls=%fused_computation.21 | convolution fusion | flops 2147745792 | bytes 8912896 | tf_op jit(solution)/shard_map/dot_general | solution.py:76
  205.5 92.8 %all-reduce.3.cloned.1.call-done = (bf16[4096,512]{1,0:T(8,128)(2,1)}, bf16[4096,512]{1,0:T(8,128)(2,1)}) async-done(((bf16[4096,512]{1,0:T(8,128)(2,1)}, bf16[4096,512]{1,0:T(8,128)(2,1)}), (bf16[4096,512]{1,0:T(8,128)(2,1)}, bf16[4096,512]{1,0:T(8,128)(2,1)})) %all-reduce.3.cloned.1.call-update) | async-done | bytes 8388624 | tf_op jit(solution)/shard_map/psum | solution.py:20
  298.3 10.5 %multiply_add_fusion = f32[512,1024]{1,0:T(8,128)} fusion(f32[512,1024]{1,0:T(8,128)S(1)} %copy-done.2, bf16[4096,512]{1,0:T(8,128)(2,1)} %all-gather.3.cloned.1.call-done, bf16[4096,512]{1,0:T(8,128)(2,1)} %get-tuple-element.5, bf16[4096,512]{1,0:T(8,128)(2,1)} %get-tuple-element.6), kind=kOutput, calls=%fused_computation.12 | convolution fusion | flops 4313317376 | bytes 16777216 | tf_op jit(solution)/shard_map/dot_general | solution.py:72
  308.9 56.4 %reduce-scatter.2.cloned.1.call-done = bf16[512,256]{1,0:T(8,128)(2,1)} async-done(((bf16[512,4096]{1,0:T(8,128)(2,1)}), bf16[512,256]{1,0:T(8,128)(2,1)}) %reduce-scatter.2.cloned.1.call-update) | async-done | bytes 262160 | tf_op jit(solution)/shard_map/reduce_scatter | solution.py:64
  365.3 1.8 multiply_add_fusion.1
  367.1 55.3 %all-gather.5.cloned.1.call-done = bf16[512,8192]{0,1:T(8,128)(2,1)} async-done(((bf16[512,512]{0,1:T(8,128)(2,1)}), bf16[512,8192]{0,1:T(8,128)(2,1)}) %all-gather.5.cloned.1.call-update) | async-done | bytes 8388624 | tf_op jit(solution)/shard_map/all_gather | solution.py:80
  422.5 11.1 %convolution_convert_fusion = bf16[512,512]{1,0:T(8,128)(2,1)} fusion(bf16[512,8192]{0,1:T(8,128)(2,1)} %all-gather.5.cloned.1.call-done, bf16[512,8192]{1,0:T(8,128)(2,1)} %param.11), kind=kOutput, calls=%fused_computation.19 | convolution fusion | flops 4295229440 | bytes 17301504 | tf_op jit(solution)/shard_map/dot_general | solution.py:79
  (23 shorter events, 2.6 us)
Async XLA Ops:
  32.2 23.7 %all-to-all-start = ((bf16[64,16,512]{2,0,1:T(8,128)(2,1)}), bf16[64,16,512]{2,0,1:T(8,128)(2,1)S(1)}, u32[]{:S(2)}, u32[]{:S(2)}) async-start(bf16[64,16,512]{2,0,1:T(8,128)(2,1)} %copy.13), calls=%async_computation | async-start | bytes 2097152 | tf_op jit(solution)/shard_map/all_to_all | solution.py:39
  40.0 89.7 %all-gather.3.cloned.1.call-start = ((), (), s32[]{:S(2)}) async-start(), calls=%async_computation.2 | async-start | bytes 4718592 | tf_op jit(solution)/shard_map/all_gather | solution.py:42
  58.8 239.5 %all-reduce.3.cloned.1.call-start = ((), (), s32[]{:S(2)}) async-start(), calls=%async_computation.5 | async-start | bytes 16777216 | tf_op jit(solution)/shard_map/psum | solution.py:20
  135.7 1.0 copy-start
  135.8 229.5 %reduce-scatter.2.cloned.1.call-start = ((), (), s32[]{:S(2)}) async-start(), calls=%async_computation.3 | async-start | bytes 4456448 | tf_op jit(solution)/shard_map/reduce_scatter | solution.py:64
  147.1 16.5 %collective-permute-start = (bf16[512,512]{1,0:T(8,128)(2,1)}, bf16[512,512]{1,0:T(8,128)(2,1)S(1)}, u32[]{:S(2)}, u32[]{:S(2)}) collective-permute-start(bf16[512,512]{1,0:T(8,128)(2,1)} %get-tuple-element.11), channel_id=1, source_target_pairs={{80,0},{96,16},{112,32},{0,48},{16,64},{32,80},{48,96},{64,112},{8... | collective-permute-start | bytes 1572872 | tf_op jit(solution)/shard_map/ppermute | solution.py:15
  147.1 25.1 %collective-permute-start.1 = (bf16[512,512]{1,0:T(8,128)(2,1)}, bf16[512,512]{1,0:T(8,128)(2,1)}, u32[]{:S(2)}, u32[]{:S(2)}) collective-permute-start(bf16[512,512]{1,0:T(8,128)(2,1)} %get-tuple-element.10), channel_id=1, source_target_pairs={{96,0},{112,16},{0,32},{16,48},{32,64},{48,80},{64,96},{80,112},{9... | collective-permute-start | bytes 1572872 | tf_op jit(solution)/shard_map/ppermute | solution.py:15
  147.9 39.7 %collective-permute-start.2 = (bf16[512,512]{1,0:T(8,128)(2,1)}, bf16[512,512]{1,0:T(8,128)(2,1)S(1)}, u32[]{:S(2)}, u32[]{:S(2)}) collective-permute-start(bf16[512,512]{1,0:T(8,128)(2,1)} %get-tuple-element.9), channel_id=1, source_target_pairs={{112,0},{0,16},{16,32},{32,48},{48,64},{64,80},{80,96},{96,112},{1... | collective-permute-start | bytes 1572872 | tf_op jit(solution)/shard_map/ppermute | solution.py:15
  198.6 99.8 %copy-start.2 = (f32[512,1024]{1,0:T(8,128)S(1)}, f32[512,1024]{1,0:T(8,128)}, u32[]{:S(2)}) copy-start(f32[512,1024]{1,0:T(8,128)} %param.9) | copy-start | bytes 6291460
  198.6 223.9 %all-gather.5.cloned.1.call-start = ((), (), s32[]{:S(2)}) async-start(), calls=%async_computation.4 | async-start | bytes 8912896 | tf_op jit(solution)/shard_map/all_gather | solution.py:80
  298.3 67.0 %copy-start.1 = (f32[512,256]{1,0:T(8,128)S(1)}, f32[512,256]{1,0:T(8,128)}, u32[]{:S(2)}) copy-start(f32[512,256]{1,0:T(8,128)} %param.8) | copy-start | bytes 1572868
Sparse Core Ops, SparseCore 0:
  58.9 70.7 all-gather.2
  135.9 162.4 all-reduce.2
  300.7 64.4 reduce-scatter.1
  367.4 54.9 all-gather.4
where the time goes:
time: 441 us; the launch traced here: 440 us
  waiting for transfers between devices  323 us (73%)
  other arithmetic  40 us (9%)
  matrix products  33.6 us (8%)
  local copies, waits for them, and re-layouts  17.4 us (4%)
  between operations  13.9 us (3%)
  starting transfers between devices  12 us (3%)
    psum x1, waiting for transfers between devices, broadcast(): return lax.psum(block, axis)  92.8 us
    all_gather x1, waiting for transfers between devices, shards(): column_panel = lax.all_gather(grad_tile, 'row', axis=0, tiled=True)  70.9 us
    reduce_scatter x1, waiting for transfers between devices, shards(): lax.psum_scatter(left_part.astype(jnp.bfloat16), 'col', scatter_dimension...  56.4 us
    all_gather x1, waiting for transfers between devices, shards(): lax.all_gather(left_mixed, 'col', axis=1, tiled=True)  55.3 us
    ppermute x3, waiting for transfers between devices, shifted(): return lax.ppermute(block, axis, route)  33.6 us
    unnamed x6, other arithmetic  29.3 us
    all_to_all x1, waiting for transfers between devices, shards(): lax.all_to_all(held_rows, 'col', split_axis=1, concat_axis=0, tiled=True)  14 us
    dot_general x1, matrix products, shards(): lax.dot_general(lax.all_gather(left_mixed, 'col', axis=1, tiled=True), ri...  11.1 us
  transfers between devices with their start and end apart: 8, of which 8 were waited for; matrix products, arithmetic and copies ran while one was open for 10% of the time, Pallas kernels for 0%

commit v1 on v0

--- a/solution.py
+++ b/solution.py
@@ -17,7 +17,7 @@
 
 def broadcast(block, axis, source):
     block = jnp.where(lax.axis_index(axis) == source, block, jnp.zeros_like(block))
-    return lax.psum(block, axis)
+    return jnp.sum(lax.all_gather(block, axis), axis=0)
 
 
 def slot_index(row_counts, tile_rows, capacity):

time: 441 us -> 1010 us (2.29)
  waiting for transfers between devices: 323 us -> 846 us
  other arithmetic: 40 us -> 90.1 us
    all_gather x0 -> x2, waiting for transfers between devices: none -> 625 us  [broadcast(): return jnp.sum(lax.all_gather(block, axis), axis=0)]
    psum x1 -> x0, waiting for transfers between devices: 92.8 us -> none  [broadcast(): return lax.psum(block, axis)]
    reduce_sum x0 -> x2, other arithmetic: none -> 50.1 us  [broadcast(): return jnp.sum(lax.all_gather(block, axis), axis=0)]
  transfers between devices with their start and end apart: 8 -> 9, of which waited for: 8 -> 9; matrix products, arithmetic and copies ran while one was open for 10% -> 6% of each run, Pallas kernels for 0% -> 0%
where the time goes in v1:
time: 1010 us
  waiting for transfers between devices  846 us (84%)
  other arithmetic  90.1 us (9%)
  matrix products  33.5 us (3%)
  local copies, waits for them, and re-layouts  16.3 us (2%)
  between operations  13.9 us (1%)
  starting transfers between devices  12.1 us (1%)
    all_gather x2, waiting for transfers between devices, broadcast(): return jnp.sum(lax.all_gather(block, axis), axis=0)  625 us
    all_gather x1, waiting for transfers between devices, shards(): column_panel = lax.all_gather(grad_tile, 'row', axis=0, tiled=True)  70.9 us
    all_gather x1, waiting for transfers between devices, shards(): lax.all_gather(left_mixed, 'col', axis=1, tiled=True)  55.5 us
    reduce_sum x2, other arithmetic, broadcast(): return jnp.sum(lax.all_gather(block, axis), axis=0)  50.1 us
    reduce_scatter x1, waiting for transfers between devices, shards(): lax.psum_scatter(left_part.astype(jnp.bfloat16), 'col', scatter_dimension...  46.6 us
    ppermute x3, waiting for transfers between devices, shifted(): return lax.ppermute(block, axis, route)  33.6 us
    unnamed x6, other arithmetic  29.3 us
  transfers between devices with their start and end apart: 9, of which 9 were waited for; matrix products, arithmetic and copies ran while one was open for 6% of the time, Pallas kernels for 0%

profile of v1, /device:TPU:1, one launch (start us, length us, event | category | flops | bytes accessed | tf_op | source)
XLA Modules:
  0.0 1012.1 jit_solution(4132442626029043398)
XLA Ops:
  7.2 22.8 %reduce.2 = bf16[524288]{0:T(1024)(128)(2,1)S(1)} reduce(bf16[1,1,524288]{2,1,0:T(2,128)(2,1)} %param.6, bf16[]{:T(256)} %constant.94), dimensions={0,1}, to_apply=%param.6.reduce_sub_computation | reduce | bytes 2097154 | tf_op args[0]
  30.6 1.5 copy.13
  32.2 7.8 all-to-all-start
  41.8 14.0 %all-to-all-done = bf16[64,16,512]{2,0,1:T(8,128)(2,1)S(1)} async-done(((bf16[64,16,512]{2,0,1:T(8,128)(2,1)}), bf16[64,16,512]{2,0,1:T(8,128)(2,1)S(1)}, u32[]{:S(2)}, u32[]{:S(2)}) %all-to-all-start) | async-done | bytes 1048608 | tf_op jit(solution)/shard_map/all_to_all | solution.py:39
  55.9 2.0 gather_fusion
  57.8 0.9 broadcast_select_fusion.2
  58.9 70.9 %all-gather.7.cloned.1.call-done = bf16[4096,512]{1,0:T(8,128)(2,1)} async-done(((bf16[512,512]{1,0:T(8,128)(2,1)}), bf16[4096,512]{1,0:T(8,128)(2,1)}) %all-gather.7.cloned.1.call-update) | async-done | bytes 4194320 | tf_op jit(solution)/shard_map/all_gather | solution.py:42
  129.7 5.2 constant_dynamic-update-slice_fusion.1
  135.0 2.7 copy.14
  137.7 2.5 slice_bitcast_fusion
  141.0 3.0 collective-permute-start.2
  144.0 12.6 %collective-permute-done = bf16[512,512]{1,0:T(8,128)(2,1)S(1)} collective-permute-done((bf16[512,512]{1,0:T(8,128)(2,1)}, bf16[512,512]{1,0:T(8,128)(2,1)S(1)}, u32[]{:S(2)}, u32[]{:S(2)}) %collective-permute-start) | collective-permute-done | bytes 524320 | tf_op jit(solution)/shard_map/ppermute | solution.py:15
  156.7 0.9 convert_dynamic-update-slice_fusion.4
  157.6 7.7 collective-permute-done.1
  165.3 2.0 convert_dynamic-update-slice_fusion.2
  167.3 13.3 %collective-permute-done.2 = bf16[512,512]{1,0:T(8,128)(2,1)S(1)} collective-permute-done((bf16[512,512]{1,0:T(8,128)(2,1)}, bf16[512,512]{1,0:T(8,128)(2,1)S(1)}, u32[]{:S(2)}, u32[]{:S(2)}) %collective-permute-start.2) | collective-permute-done | bytes 524320 | tf_op jit(solution)/shard_map/ppermute | solution.py:15
  180.6 0.9 convert_dynamic-update-slice_fusion
  181.5 1.6 constant_dynamic-update-slice_fusion
  184.0 1.9 convert_dynamic-update-slice_fusion.3
  185.9 0.9 convert_dynamic-update-slice_fusion.1
  186.7 4.6 dynamic-slice_convert_fusion
  191.6 6.6 fusion.9
  198.3 6.0 broadcast_select_fusion.1
  204.9 46.6 %reduce-scatter.2.cloned.1.call-done = bf16[512,256]{1,0:T(8,128)(2,1)} async-done(((bf16[512,4096]{1,0:T(8,128)(2,1)}), bf16[512,256]{1,0:T(8,128)(2,1)}) %reduce-scatter.2.cloned.1.call-update) | async-done | bytes 262160 | tf_op jit(solution)/shard_map/reduce_scatter | solution.py:64
  251.5 1.8 multiply_add_fusion.1
  253.3 55.5 %all-gather.9.cloned.1.call-done = bf16[512,8192]{0,1:T(8,128)(2,1)} async-done(((bf16[512,512]{0,1:T(8,128)(2,1)}), bf16[512,8192]{0,1:T(8,128)(2,1)}) %all-gather.9.cloned.1.call-update) | async-done | bytes 8388624 | tf_op jit(solution)/shard_map/all_gather | solution.py:80
  308.8 11.1 %convolution_convert_fusion = bf16[512,512]{1,0:T(8,128)(2,1)} fusion(bf16[512,8192]{0,1:T(8,128)(2,1)} %all-gather.9.cloned.1.call-done, bf16[512,8192]{1,0:T(8,128)(2,1)} %param.11), kind=kOutput, calls=%fused_computation.19 | convolution fusion | flops 4295229440 | bytes 17301504 | tf_op jit(solution)/shard_map/dot_general | solution.py:79
  319.9 320.2 %all-gather.11.cloned.1.call-done = bf16[65536,512]{1,0:T(8,128)(2,1)} async-done(((bf16[4096,512]{1,0:T(8,128)(2,1)}), bf16[65536,512]{1,0:T(8,128)(2,1)}) %all-gather.11.cloned.1.call-update) | async-done | bytes 67108880 | tf_op jit(solution)/shard_map/all_gather | solution.py:20
  640.1 26.4 %reduce_sum.34 = bf16[4096,512]{1,0:T(8,128)(2,1)} reduce(bf16[16,4096,512]{2,1,0:T(8,128)(2,1)} %bitcast.9, bf16[]{:T(256)} %constant.90.clone.1), dimensions={0}, to_apply=%region_4.5 | reduce | flops 31457280 | bytes 71303168 | tf_op jit(solution)/shard_map/reduce_sum | solution.py:20
  666.4 304.9 %all-gather.13.cloned.1.call-done = bf16[65536,512]{1,0:T(8,128)(2,1)} async-done(((bf16[4096,512]{1,0:T(8,128)(2,1)}), bf16[65536,512]{1,0:T(8,128)(2,1)}) %all-gather.13.cloned.1.call-update) | async-done | bytes 67108880 | tf_op jit(solution)/shard_map/all_gather | solution.py:20
  971.3 23.7 %reduce_sum.35 = bf16[4096,512]{1,0:T(8,128)(2,1)} reduce(bf16[16,4096,512]{2,1,0:T(8,128)(2,1)} %bitcast.10, bf16[]{:T(256)} %constant.90.clone.1), dimensions={0}, to_apply=%region_5.6 | reduce | flops 31457280 | bytes 71303168 | tf_op jit(solution)/shard_map/reduce_sum | solution.py:20
  995.1 10.5 %multiply_add_fusion = f32[512,1024]{1,0:T(8,128)} fusion(f32[512,1024]{1,0:T(8,128)S(1)} %copy-done.1, bf16[4096,512]{1,0:T(8,128)(2,1)} %all-gather.7.cloned.1.call-done, bf16[4096,512]{1,0:T(8,128)(2,1)} %reduce_sum.35, bf16[4096,512]{1,0:T(8,128)(2,1)} %reduce_sum.34), kind=kOutput, calls=%fused_computation.12 | convolution fusion | flops 4313317376 | bytes 16777216 | tf_op jit(solution)/shard_map/dot_general | solution.py:72
  (26 shorter events, 5.0 us)
Async XLA Ops:
  32.2 23.7 %all-to-all-start = ((bf16[64,16,512]{2,0,1:T(8,128)(2,1)}), bf16[64,16,512]{2,0,1:T(8,128)(2,1)S(1)}, u32[]{:S(2)}, u32[]{:S(2)}) async-start(bf16[64,16,512]{2,0,1:T(8,128)(2,1)} %copy.13), calls=%async_computation | async-start | bytes 2097152 | tf_op jit(solution)/shard_map/all_to_all | solution.py:39
  40.0 89.7 %all-gather.7.cloned.1.call-start = ((), (), s32[]{:S(2)}) async-start(), calls=%async_computation.2 | async-start | bytes 4718592 | tf_op jit(solution)/shard_map/all_gather | solution.py:42
  58.8 192.7 %reduce-scatter.2.cloned.1.call-start = ((), (), s32[]{:S(2)}) async-start(), calls=%async_computation.3 | async-start | bytes 4456448 | tf_op jit(solution)/shard_map/reduce_scatter | solution.py:64
  140.2 16.5 %collective-permute-start = (bf16[512,512]{1,0:T(8,128)(2,1)}, bf16[512,512]{1,0:T(8,128)(2,1)S(1)}, u32[]{:S(2)}, u32[]{:S(2)}) collective-permute-start(bf16[512,512]{1,0:T(8,128)(2,1)} %get-tuple-element.9), channel_id=1, source_target_pairs={{80,0},{96,16},{112,32},{0,48},{16,64},{32,80},{48,96},{64,112},{8... | collective-permute-start | bytes 1572872 | tf_op jit(solution)/shard_map/ppermute | solution.py:15
  140.2 25.1 %collective-permute-start.1 = (bf16[512,512]{1,0:T(8,128)(2,1)}, bf16[512,512]{1,0:T(8,128)(2,1)}, u32[]{:S(2)}, u32[]{:S(2)}) collective-permute-start(bf16[512,512]{1,0:T(8,128)(2,1)} %get-tuple-element.8), channel_id=1, source_target_pairs={{96,0},{112,16},{0,32},{16,48},{32,64},{48,80},{64,96},{80,112},{9... | collective-permute-start | bytes 1572872 | tf_op jit(solution)/shard_map/ppermute | solution.py:15
  141.0 39.6 %collective-permute-start.2 = (bf16[512,512]{1,0:T(8,128)(2,1)}, bf16[512,512]{1,0:T(8,128)(2,1)S(1)}, u32[]{:S(2)}, u32[]{:S(2)}) collective-permute-start(bf16[512,512]{1,0:T(8,128)(2,1)} %get-tuple-element.7), channel_id=1, source_target_pairs={{112,0},{0,16},{16,32},{32,48},{48,64},{64,80},{80,96},{96,112},{1... | collective-permute-start | bytes 1572872 | tf_op jit(solution)/shard_map/ppermute | solution.py:15
  191.4 117.5 %all-gather.9.cloned.1.call-start = ((), (), s32[]{:S(2)}) async-start(), calls=%async_computation.4 | async-start | bytes 8912896 | tf_op jit(solution)/shard_map/all_gather | solution.py:80
  198.2 441.8 %all-gather.11.cloned.1.call-start = ((), (), s32[]{:S(2)}) async-start(), calls=%async_computation.5 | async-start | bytes 71303168 | tf_op jit(solution)/shard_map/all_gather | solution.py:20
  204.3 47.2 %copy-start = (f32[512,256]{1,0:T(8,128)S(1)}, f32[512,256]{1,0:T(8,128)}, u32[]{:S(2)}) copy-start(f32[512,256]{1,0:T(8,128)} %param.8) | copy-start | bytes 1572868
  204.3 767.0 %all-gather.13.cloned.1.call-start = ((), (), s32[]{:S(2)}) async-start(), calls=%async_computation.6 | async-start | bytes 71303168 | tf_op jit(solution)/shard_map/all_gather | solution.py:20
  971.3 23.7 %copy-start.1 = (f32[512,1024]{1,0:T(8,128)S(1)}, f32[512,1024]{1,0:T(8,128)}, u32[]{:S(2)}) copy-start(f32[512,1024]{1,0:T(8,128)} %param.9) | copy-start | bytes 6291460
Sparse Core Ops, SparseCore 0:
  58.9 70.7 all-gather.6
  191.5 59.9 reduce-scatter.1
  253.8 54.9 all-gather.8
  310.4 329.6 all-gather.10
  641.6 329.6 all-gather.12
